TPU v7x, 128 devices: a whole 4x4x4 slice. The times are simulated.
128 devices in a mesh: hot: 4 (over z), dom: 32 (over y, x, core).
Axes of the slice: x: 4, y: 4, z: 4, core: 2. Of those that a mesh axis runs over, the one named last changes fastest.
Arguments:
- macro_adjoint: float32 [16, 6], P('hot'), may hold values from -6 to 6
- slip_code: int32 [32, 64, 4096], P('hot', 'dom'), may hold values from 0 to 4095
- grain_id: int32 [32, 64, 4096], P('hot', 'dom'), may hold values from 0 to 63
- grain_modulus: float32 [64], replicated, may hold values from 0.5 to 4
- slip_softening: float32 [64, 12], replicated, may hold values from 0.1 to 1.5
- rve_spot: int32 [32], P('hot'), may hold values from 0 to 15, as said below
Outputs:
- sensitivity: float32 [16, 6], P('hot')
- adjoint_field: float32 [32, 3, 64, 4096], P('hot', None, 'dom')
Inputs may be any that keep to these rules, and one draw needn't show every extreme that they name: `rve_spot`: every hot-spot is named by exactly 2 RVEs.
All inputs are finite; a program needn't handle non-finite values.
Results may differ from a plain program's by a relative error of at most 0.0003.
Values sent between devices are 32-bit elements; how exact they have to be, the bound alone decides.
No kernel may reach another device: no remote copies, remote signals or barrier semaphores. Data moves between devices by JAX's collectives and lax.ppermute only.
A program may use at most 64 MiB of HBM per device.

v0:
```python
import jax
import jax.numpy as jnp
from jax import lax
from jax.sharding import PartitionSpec as P

RES = 64
SLIPS = 12
GRAINS = 64
ITERS = 8


mass_term = 0.02


def padded_2(value, sides, width):
    for axis, dim in sides:
        devices, length = (lax.axis_size(axis), value.shape[dim])
        up = [(i, (i + 1) % devices) for i in range(devices - 1)]
        down = [(j, i) for i, j in up]
        last = lax.slice_in_dim(value, length - width, length, axis=dim)
        leading = lax.slice_in_dim(value, 0, width, axis=dim)
        before = lax.ppermute(last, axis, up)
        after = lax.ppermute(leading, axis, down)
        value = jnp.concatenate([before, value, after], axis=dim)
    return value


def shift_cells(field, step):
    filler = jnp.zeros(field.shape[:-1] + (abs(step),), field.dtype)
    if step > 0:
        return jnp.concatenate([field[..., step:], filler], -1)
    return jnp.concatenate([filler, field[..., :step]], -1)


def local_dot(first, second):
    return jnp.sum(first * second, axis=(1, 2, 3))


def shards(macro_adjoint, slip_code, grain_id, grain_modulus, slip_softening, rve_spot):
    rve_count = slip_code.shape[0]
    cells = slip_code.shape[2]
    spot_count = macro_adjoint.shape[0] * lax.axis_size("hot")
    column = jnp.arange(cells) % RES
    upper_mask = (column != RES - 1).astype(jnp.float32)
    lower_mask = (column != 0).astype(jnp.float32)
    table = jnp.concatenate([grain_modulus[None, :], slip_softening.T], 0)

    def stiff_one(inputs):
        codes, grain_cells = inputs
        flat_codes = codes.reshape(-1)
        flat_grains = grain_cells.reshape(-1)
        onehot = (jnp.arange(GRAINS)[:, None] == flat_grains[None, :]).astype(jnp.float32)
        looked = jnp.dot(
            table, onehot, precision=lax.Precision.HIGHEST, preferred_element_type=jnp.float32
        )
        softening = jnp.zeros(flat_codes.shape, jnp.float32)
        for slip in range(SLIPS):
            active = (flat_codes // 2**slip % 2).astype(jnp.float32)
            softening = softening + active * looked[1 + slip]
        return (looked[0] / (1.0 + softening)).reshape(codes.shape)

    all_strains = lax.all_gather(macro_adjoint, "hot", axis=0, tiled=True)
    spot_onehot = (rve_spot[:, None] == jnp.arange(spot_count)[None, :]).astype(jnp.float32)
    strains = jnp.dot(
        spot_onehot,
        all_strains,
        precision=lax.Precision.HIGHEST,
        preferred_element_type=jnp.float32,
    )
    stiff = lax.map(stiff_one, (slip_code, grain_id))
    padded = padded_2(stiff, (("dom", 1),), 1)

    def squares(residual):
        return lax.psum(local_dot(residual, residual), "dom")

    near_xup = padded[:, 2:]
    near_xdn = padded[:, :-2]
    near_yup = shift_cells(stiff, RES)
    near_ydn = shift_cells(stiff, -RES)
    near_zup = shift_cells(stiff, 1) * upper_mask
    near_zdn = shift_cells(stiff, -1) * lower_mask
    face_xup = 0.5 * (stiff + near_xup)
    face_xdn = 0.5 * (stiff + near_xdn)
    face_yup = 0.5 * (stiff + near_yup)
    face_ydn = 0.5 * (stiff + near_ydn)
    face_zup = 0.5 * (stiff + near_zup)
    face_zdn = 0.5 * (stiff + near_zdn)
    diagonal_sum = (mass_term + face_xup + face_xdn + face_yup + face_ydn + face_zup + face_zdn)[
        :, None
    ]
    gradients = [
        0.5 * (near_xup - near_xdn),
        0.5 * (near_yup - near_ydn),
        0.5 * (near_zup - near_zdn),
    ]
    tensor = [
        [strains[:, 0], strains[:, 5], strains[:, 4]],
        [strains[:, 5], strains[:, 1], strains[:, 3]],
        [strains[:, 4], strains[:, 3], strains[:, 2]],
    ]
    source = jnp.stack(
        [
            gradients[0] * tensor[comp][0][:, None, None]
            + gradients[1] * tensor[comp][1][:, None, None]
            + gradients[2] * tensor[comp][2][:, None, None]
            for comp in range(3)
        ],
        1,
    )

    def expand(values):
        return values[:, None, None, None]

    answer = jnp.zeros_like(source)
    residual = source
    direction = source
    norm_now = squares(residual)
    for step in range(ITERS):
        wide = padded_2(direction, (("dom", 2),), 1)
        image = (
            diagonal_sum * direction
            - face_xup[:, None] * wide[:, :, 2:]
            - face_xdn[:, None] * wide[:, :, :-2]
            - face_yup[:, None] * shift_cells(direction, RES)
            - face_ydn[:, None] * shift_cells(direction, -RES)
            - face_zup[:, None] * (shift_cells(direction, 1) * upper_mask)
            - face_zdn[:, None] * (shift_cells(direction, -1) * lower_mask)
        )
        alpha = norm_now / lax.psum(local_dot(direction, image), "dom")
        answer = answer + expand(alpha) * direction
        residual = residual - expand(alpha) * image
        norm_next = squares(residual)
        direction = residual + expand(norm_next / norm_now) * direction
        norm_now = norm_next
    volume = float(RES**3)
    stiff_part = jnp.sum(stiff, axis=(1, 2)) / volume
    moment = [
        [jnp.sum(answer[:, comp] * gradients[other], axis=(1, 2)) for other in range(3)]
        for comp in range(3)
    ]
    pairs = [(0, 0), (1, 1), (2, 2), (1, 2), (0, 2), (0, 1)]
    partial_here = jnp.stack(
        [
            stiff_part * strains[:, slot]
            - 0.5
            * (moment[pairs[slot][0]][pairs[slot][1]] + moment[pairs[slot][1]][pairs[slot][0]])
            / volume
            for slot in range(6)
        ],
        1,
    )
    per_spot = float(rve_count * lax.axis_size("hot") // spot_count)
    rve_totals = lax.psum(partial_here, "dom")
    spot_local = jnp.dot(
        spot_onehot.T,
        rve_totals,
        precision=lax.Precision.HIGHEST,
        preferred_element_type=jnp.float32,
    )
    owned = lax.psum_scatter(spot_local, "hot", scatter_dimension=0, tiled=True)
    return (owned / per_spot, answer)


def solution(mesh):
    return jax.shard_map(
        shards,
        mesh=mesh,
        in_specs=(P("hot", None), P("hot", "dom", None), P("hot", "dom", None), P(), P(), P("hot")),
        out_specs=(P("hot", None), P("hot", None, "dom", None)),
        check_vma=False,
    )
```

profile of v0, /device:TPU:0, one launch (start us, length us, event | category | flops | bytes accessed | tf_op | source)
XLA Modules:
  0.0 1254.9 jit_solution(1973612798460784764)
XLA Ops:
  1.3 40.5 %while.13 = (s32[]{:T(128)}, f32[8,2,4096]{2,1,0:T(2,128)S(1)}, s32[8,2,4096]{2,1,0:T(2,128)}, f32[13,64]{1,0:T(8,128)S(1)}, s32[8,2,4096]{2,1,0:T(2,128)}, /*index=5*/s32[]{:T(128)}) while((s32[]{:T(128)}, f32[8,2,4096]{2,1,0:T(2,128)S(1)}, s32[8,2,4096]{2,1,0:T(2,128)}, f32[13,64]{1,0:T(8,128)S(1)}, s32[8,2,4096]{2,1,0:T(2,128)}, ...), condition=%wide.region_1.2_spmd, body=%wide.region_0.1_spmd.sunk | while | flops 84582400 | bytes 2788685 | solution.py:70
  4.3 2.1 divide_dynamic-update-slice_fusion.2
  9.4 2.1 divide_dynamic-update-slice_fusion.2
  14.4 2.1 divide_dynamic-update-slice_fusion.2
  19.5 2.1 divide_dynamic-update-slice_fusion.2
  24.6 2.1 divide_dynamic-update-slice_fusion.2
  29.6 2.1 divide_dynamic-update-slice_fusion.2
  34.7 2.1 divide_dynamic-update-slice_fusion.2
  39.7 2.1 divide_dynamic-update-slice_fusion.2
  42.1 1.3 collective-permute-start
  43.4 3.0 collective-permute-start.1
  47.5 12.1 all-gather
  66.5 3.2 collective-permute-start.3
  69.8 1.4 add_add_fusion
  71.3 5.7 multiply_reduce_fusion.14
  77.0 67.4 %all-reduce.37 = (f32[8]{0:T(128)S(1)}, f32[8]{0:T(128)S(1)}) all-reduce(f32[8]{0:T(128)S(1)} %get-tuple-element.148, f32[8]{0:T(128)S(1)} %get-tuple-element.147), channel_id=1, replica_groups=mesh['hot'=4,'dom'=32] {'dom'}, use_global_device_ids=true, to_apply=%region_4.5 | all-reduce | flops 16 | bytes 128 | tf_op jit(solution)/shard_map/psum | solution.py:74
  144.4 1.9 multiply_reduce_fusion.13
  146.3 62.9 %psum.121 = f32[8]{0:T(128)S(1)} all-reduce(f32[8]{0:T(128)S(1)} %get-tuple-element.185), channel_id=1, replica_groups=mesh['hot'=4,'dom'=32] {'dom'}, use_global_device_ids=true, to_apply=%region_8.9 | all-reduce | flops 8 | bytes 64 | tf_op jit(solution)/shard_map/psum | solution.py:74
  209.3 1.7 multiply_add_fusion.7
  214.1 3.1 collective-permute-start.5
  218.4 5.4 multiply_reduce_fusion.12
  223.8 66.8 %psum.122 = f32[8]{0:T(128)S(1)} all-reduce(f32[8]{0:T(128)S(1)} %get-tuple-element.183), channel_id=1, replica_groups=mesh['hot'=4,'dom'=32] {'dom'}, use_global_device_ids=true, to_apply=%region_10.11 | all-reduce | flops 8 | bytes 64 | tf_op jit(solution)/shard_map/psum | solution.py:129
  290.7 2.7 multiply_reduce_fusion.11
  293.4 62.7 %psum.123 = f32[8]{0:T(128)S(1)} all-reduce(f32[8]{0:T(128)S(1)} %get-tuple-element.181), channel_id=1, replica_groups=mesh['hot'=4,'dom'=32] {'dom'}, use_global_device_ids=true, to_apply=%region_12.13 | all-reduce | flops 8 | bytes 64 | tf_op jit(solution)/shard_map/psum | solution.py:74
  356.0 2.3 multiply_add_fusion.6
  360.1 1.3 collective-permute-start.6
  361.4 3.3 collective-permute-start.7
  365.8 5.4 multiply_reduce_fusion.10
  371.2 67.1 %psum.124 = f32[8]{0:T(128)S(1)} all-reduce(f32[8]{0:T(128)S(1)} %get-tuple-element.179), channel_id=1, replica_groups=mesh['hot'=4,'dom'=32] {'dom'}, use_global_device_ids=true, to_apply=%region_14.15 | all-reduce | flops 8 | bytes 64 | tf_op jit(solution)/shard_map/psum | solution.py:129
  438.3 2.6 multiply_reduce_fusion.9
  440.9 62.7 %psum.125 = f32[8]{0:T(128)S(1)} all-reduce(f32[8]{0:T(128)S(1)} %get-tuple-element.177), channel_id=1, replica_groups=mesh['hot'=4,'dom'=32] {'dom'}, use_global_device_ids=true, to_apply=%region_16.17 | all-reduce | flops 8 | bytes 64 | tf_op jit(solution)/shard_map/psum | solution.py:74
  503.6 1.6 multiply_add_fusion.5
  508.3 3.1 collective-permute-start.9
  512.6 5.4 multiply_reduce_fusion.8
  518.1 67.1 %psum.126 = f32[8]{0:T(128)S(1)} all-reduce(f32[8]{0:T(128)S(1)} %get-tuple-element.175), channel_id=1, replica_groups=mesh['hot'=4,'dom'=32] {'dom'}, use_global_device_ids=true, to_apply=%region_18.19 | all-reduce | flops 8 | bytes 64 | tf_op jit(solution)/shard_map/psum | solution.py:129
  585.2 2.8 multiply_reduce_fusion.7
  588.0 62.7 %psum.127 = f32[8]{0:T(128)S(1)} all-reduce(f32[8]{0:T(128)S(1)} %get-tuple-element.173), channel_id=1, replica_groups=mesh['hot'=4,'dom'=32] {'dom'}, use_global_device_ids=true, to_apply=%region_20.21 | all-reduce | flops 8 | bytes 64 | tf_op jit(solution)/shard_map/psum | solution.py:74
  650.7 1.6 multiply_add_fusion.4
  655.4 3.6 collective-permute-start.11
  660.0 5.5 multiply_reduce_fusion.6
  665.5 67.1 %psum.128 = f32[8]{0:T(128)S(1)} all-reduce(f32[8]{0:T(128)S(1)} %get-tuple-element.171), channel_id=1, replica_groups=mesh['hot'=4,'dom'=32] {'dom'}, use_global_device_ids=true, to_apply=%region_22.23 | all-reduce | flops 8 | bytes 64 | tf_op jit(solution)/shard_map/psum | solution.py:129
  732.6 2.8 multiply_reduce_fusion.5
  735.4 62.7 %psum.129 = f32[8]{0:T(128)S(1)} all-reduce(f32[8]{0:T(128)S(1)} %get-tuple-element.169), channel_id=1, replica_groups=mesh['hot'=4,'dom'=32] {'dom'}, use_global_device_ids=true, to_apply=%region_24.25 | all-reduce | flops 8 | bytes 64 | tf_op jit(solution)/shard_map/psum | solution.py:74
  798.1 1.6 multiply_add_fusion.3
  801.5 1.3 collective-permute-start.12
  802.8 3.2 collective-permute-start.13
  807.4 5.5 multiply_reduce_fusion.4
  812.9 67.1 %psum.130 = f32[8]{0:T(128)S(1)} all-reduce(f32[8]{0:T(128)S(1)} %get-tuple-element.167), channel_id=1, replica_groups=mesh['hot'=4,'dom'=32] {'dom'}, use_global_device_ids=true, to_apply=%region_26.27 | all-reduce | flops 8 | bytes 64 | tf_op jit(solution)/shard_map/psum | solution.py:129
  880.0 2.8 multiply_reduce_fusion.3
  882.8 62.7 %psum.131 = f32[8]{0:T(128)S(1)} all-reduce(f32[8]{0:T(128)S(1)} %get-tuple-element.165), channel_id=1, replica_groups=mesh['hot'=4,'dom'=32] {'dom'}, use_global_device_ids=true, to_apply=%region_28.29 | all-reduce | flops 8 | bytes 64 | tf_op jit(solution)/shard_map/psum | solution.py:74
  945.5 1.6 multiply_add_fusion.2
  950.3 3.4 collective-permute-start.15
  954.8 5.5 multiply_reduce_fusion.2
  960.4 67.1 %psum.132 = f32[8]{0:T(128)S(1)} all-reduce(f32[8]{0:T(128)S(1)} %get-tuple-element.163), channel_id=1, replica_groups=mesh['hot'=4,'dom'=32] {'dom'}, use_global_device_ids=true, to_apply=%region_30.31 | all-reduce | flops 8 | bytes 64 | tf_op jit(solution)/shard_map/psum | solution.py:129
  1027.5 2.8 multiply_reduce_fusion.1
  1030.3 62.7 %psum.133 = f32[8]{0:T(128)S(1)} all-reduce(f32[8]{0:T(128)S(1)} %get-tuple-element.161), channel_id=1, replica_groups=mesh['hot'=4,'dom'=32] {'dom'}, use_global_device_ids=true, to_apply=%region_32.33 | all-reduce | flops 8 | bytes 64 | tf_op jit(solution)/shard_map/psum | solution.py:74
  1093.0 5.2 multiply_add_fusion.1
  1101.3 3.2 collective-permute-start.17
  1105.8 4.3 multiply_reduce_fusion
  1110.7 67.1 %psum.134 = f32[8]{0:T(128)S(1)} all-reduce(f32[8]{0:T(128)S(1)} %multiply_reduce_fusion), channel_id=1, replica_groups=mesh['hot'=4,'dom'=32] {'dom'}, use_global_device_ids=true, to_apply=%region_34.35 | all-reduce | flops 8 | bytes 64 | tf_op jit(solution)/shard_map/psum | solution.py:129
  1177.9 1.7 copy_add_fusion
  1179.7 1.4 multiply_reduce_fusion.16
  1181.1 62.7 %psum.135 = f32[8,6]{0,1:T(8,128)S(1)} all-reduce(f32[8,6]{0,1:T(8,128)S(1)} %stack.25), channel_id=1, replica_groups=mesh['hot'=4,'dom'=32] {'dom'}, use_global_device_ids=true, to_apply=%region_44.45 | all-reduce | flops 48 | bytes 384 | tf_op jit(solution)/shard_map/psum | solution.py:153
  1244.1 10.0 all-reduce.36
  (335 shorter events, 60.0 us)
Async XLA Ops:
  42.1 18.4 %collective-permute-start = (f32[8,1,4096]{2,1,0:T(1,128)S(1)}, f32[8,1,4096]{2,1,0:T(1,128)S(1)}, u32[]{:S(2)}, u32[]{:S(2)}) collective-permute-start(f32[8,1,4096]{2,1,0:T(1,128)S(1)} %get-tuple-element.256), channel_id=1, source_target_pairs={{1,0},{2,1},{3,2},{4,3},{5,4},{6,5},{7,6},{8,7},{9,8},{10,9},{11,1... | collective-permute-start | bytes 393224 | tf_op jit(solution)/shard_map/ppermute | solution.py:23
  43.4 17.1 %collective-permute-start.1 = (f32[8,1,4096]{2,1,0:T(1,128)S(1)}, f32[8,1,4096]{2,1,0:T(1,128)S(1)}, u32[]{:S(2)}, u32[]{:S(2)}) collective-permute-start(f32[8,1,4096]{2,1,0:T(1,128)S(1)} %get-tuple-element.257), channel_id=1, source_target_pairs={{0,1},{1,2},{2,3},{3,4},{4,5},{5,6},{6,7},{7,8},{8,9},{9,10},{10,1... | collective-permute-start | bytes 393224 | tf_op jit(solution)/shard_map/ppermute | solution.py:22
  46.7 14.8 %copy-start.45 = (f32[8,2,4095]{2,1,0:T(2,128)}, f32[8,2,4095]{2,1,0:T(2,128)S(1)}, u32[]{:S(2)}) copy-start(f32[8,2,4095]{2,1,0:T(2,128)S(1)} %get-tuple-element.252) | copy-start | bytes 786244
  46.8 14.8 %copy-start.47 = (f32[8,2,4095]{2,1,0:T(2,128)}, f32[8,2,4095]{2,1,0:T(2,128)S(1)}, u32[]{:S(2)}) copy-start(f32[8,2,4095]{2,1,0:T(2,128)S(1)} %get-tuple-element.253) | copy-start | bytes 786244
  46.8 12.8 %copy-start.58 = (s32[8]{0:T(128)S(1)}, s32[8]{0:T(128)}, u32[]{:S(2)}) copy-start(s32[8]{0:T(128)} %param.13) | copy-start | bytes 100
  46.8 13.0 %copy-start.59 = (u32[128]{0:T(128)S(1)}, u32[128]{0:T(128)}, u32[]{:S(2)}) copy-start(u32[128]{0:T(128)} %constant.499) | copy-start | bytes 1540
  47.1 14.4 %copy-start.49 = (f32[8,2,4032]{2,1,0:T(2,128)}, f32[8,2,4032]{2,1,0:T(2,128)S(1)}, u32[]{:S(2)}) copy-start(f32[8,2,4032]{2,1,0:T(2,128)S(1)} %get-tuple-element.254) | copy-start | bytes 774148
  47.1 14.4 %copy-start.51 = (f32[8,2,4032]{2,1,0:T(2,128)}, f32[8,2,4032]{2,1,0:T(2,128)S(1)}, u32[]{:S(2)}) copy-start(f32[8,2,4032]{2,1,0:T(2,128)S(1)} %get-tuple-element.255) | copy-start | bytes 774148
  61.6 82.8 %copy-start.30 = (f32[8,1,2,4096]{3,2,0,1:T(2,128)}, f32[8,1,2,4096]{3,2,0,1:T(2,128)S(1)}, u32[]{:S(2)}) copy-start(f32[8,1,2,4096]{3,2,0,1:T(2,128)S(1)} %get-tuple-element.195) | copy-start | bytes 786436
  62.1 82.4 %copy-start.32 = (f32[8,1,2,4096]{3,2,0,1:T(2,128)}, f32[8,1,2,4096]{3,2,0,1:T(2,128)S(1)}, u32[]{:S(2)}) copy-start(f32[8,1,2,4096]{3,2,0,1:T(2,128)S(1)} %get-tuple-element.199) | copy-start | bytes 786436
  62.1 82.3 %copy-start.34 = (f32[8,1,2,4096]{3,2,0,1:T(2,128)}, f32[8,1,2,4096]{3,2,0,1:T(2,128)S(1)}, u32[]{:S(2)}) copy-start(f32[8,1,2,4096]{3,2,0,1:T(2,128)S(1)} %get-tuple-element.200) | copy-start | bytes 786436
  64.3 5.5 copy-start.46
  64.3 5.5 copy-start.48
  64.3 5.5 copy-start.50
  64.3 5.5 copy-start.52
  64.3 5.5 copy-start.54
  64.4 5.5 copy-start.56
  65.2 6.0 collective-permute-start.2
  66.5 4.7 collective-permute-start.3
  71.2 441.4 %copy-start.14 = (f32[8,2,4096]{2,1,0:T(2,128)}, f32[8,2,4096]{2,1,0:T(2,128)S(1)}, u32[]{:S(2)}) copy-start(f32[8,2,4096]{2,1,0:T(2,128)S(1)} %get-tuple-element.192) | copy-start | bytes 786436
  71.2 441.4 %copy-start.19 = (f32[8,2,4096]{2,1,0:T(2,128)}, f32[8,2,4096]{2,1,0:T(2,128)S(1)}, u32[]{:S(2)}) copy-start(f32[8,2,4096]{2,1,0:T(2,128)S(1)} %get-tuple-element.193) | copy-start | bytes 786436
  71.2 441.4 %copy-start.24 = (f32[8,2,4096]{2,1,0:T(2,128)}, f32[8,2,4096]{2,1,0:T(2,128)S(1)}, u32[]{:S(2)}) copy-start(f32[8,2,4096]{2,1,0:T(2,128)S(1)} %get-tuple-element.194) | copy-start | bytes 786436
  71.2 588.7 %copy-start.2 = (f32[8,2,4096]{2,1,0:T(2,128)}, f32[8,2,4096]{2,1,0:T(2,128)S(1)}, u32[]{:S(2)}) copy-start(f32[8,2,4096]{2,1,0:T(2,128)S(1)} %get-tuple-element.189) | copy-start | bytes 786436
  71.2 588.7 %copy-start.6 = (f32[8,2,4096]{2,1,0:T(2,128)}, f32[8,2,4096]{2,1,0:T(2,128)S(1)}, u32[]{:S(2)}) copy-start(f32[8,2,4096]{2,1,0:T(2,128)S(1)} %get-tuple-element.190) | copy-start | bytes 786436
  71.2 588.7 %copy-start.10 = (f32[8,2,4096]{2,1,0:T(2,128)}, f32[8,2,4096]{2,1,0:T(2,128)S(1)}, u32[]{:S(2)}) copy-start(f32[8,2,4096]{2,1,0:T(2,128)S(1)} %get-tuple-element.191) | copy-start | bytes 786436
  146.3 144.3 %copy-start.29 = (f32[8,3,2,4096]{3,2,0,1:T(2,128)}, f32[8,3,2,4096]{3,2,0,1:T(2,128)S(1)}, u32[]{:S(2)}) copy-start(f32[8,3,2,4096]{3,2,0,1:T(2,128)S(1)} %get-tuple-element.186) | copy-start | bytes 2359300
  212.8 5.3 collective-permute-start.4
  214.1 4.4 collective-permute-start.5
  290.7 65.3 %copy-start.31 = (f32[8,1,2,4096]{3,2,0,1:T(2,128)S(1)}, f32[8,1,2,4096]{3,2,0,1:T(2,128)}, u32[]{:S(2)}) copy-start(f32[8,1,2,4096]{3,2,0,1:T(2,128)} %copy-done.30) | copy-start | bytes 786436
  290.7 65.4 %copy-start.33 = (f32[8,1,2,4096]{3,2,0,1:T(2,128)S(1)}, f32[8,1,2,4096]{3,2,0,1:T(2,128)}, u32[]{:S(2)}) copy-start(f32[8,1,2,4096]{3,2,0,1:T(2,128)} %copy-done.32) | copy-start | bytes 786436
  290.7 65.3 %copy-start.35 = (f32[8,1,2,4096]{3,2,0,1:T(2,128)S(1)}, f32[8,1,2,4096]{3,2,0,1:T(2,128)}, u32[]{:S(2)}) copy-start(f32[8,1,2,4096]{3,2,0,1:T(2,128)} %copy-done.34) | copy-start | bytes 786436
  360.1 5.5 collective-permute-start.6
  361.4 4.4 collective-permute-start.7
  365.8 72.5 %copy-start.36 = (f32[8,3,2,4096]{3,2,0,1:T(2,128)S(1)}, f32[8,3,2,4096]{3,2,0,1:T(2,128)}, u32[]{:S(2)}) copy-start(f32[8,3,2,4096]{3,2,0,1:T(2,128)} %get-tuple-element.182) | copy-start | bytes 2359300
  507.0 5.3 collective-permute-start.8
  508.3 4.4 collective-permute-start.9
  654.1 5.8 collective-permute-start.10
  655.4 4.6 copy-start.15
  655.4 4.6 copy-start.20
  655.4 4.6 copy-start.25
  655.4 4.5 collective-permute-start.11
  801.5 5.5 collective-permute-start.12
  802.8 4.6 copy-start.3
  802.8 4.6 copy-start.7
  802.8 4.5 copy-start.11
  802.8 4.5 collective-permute-start.13
  947.1 7.6 copy-start.1
  948.9 5.6 collective-permute-start.14
  950.2 4.6 copy-start.4
  950.2 4.6 copy-start.8
  950.2 4.6 copy-start.12
  950.2 4.5 copy-start.17
  950.2 4.5 copy-start.22
  950.3 4.5 copy-start.27
  950.3 4.5 collective-permute-start.15
  1098.1 7.6 copy-start
  1099.9 5.5 collective-permute-start.16
  1101.2 4.6 copy-start.5
  1101.2 4.6 copy-start.9
  1101.2 4.6 copy-start.13
  1101.2 4.5 copy-start.18
  1101.3 4.5 copy-start.23
  1101.3 4.5 collective-permute-start.17
  1105.8 72.1 %copy-start.37 = (f32[8,3,2,4096]{3,2,0,1:T(2,128)S(1)}, f32[8,3,2,4096]{3,2,0,1:T(2,128)}, u32[]{:S(2)}) copy-start(f32[8,3,2,4096]{3,2,0,1:T(2,128)} %get-tuple-element.201) | copy-start | bytes 2359300
  (14 other events, 30.5 us)
where the time goes:
time: 1260 us; the launch traced here: 1250 us
  blocking collectives  1060 us (84%)
  other arithmetic  101 us (8%)
  starting transfers between devices  40.6 us (3%)
  local copies, waits for them, and re-layouts  40.4 us (3%)
    psum x8, blocking collectives, squares(): return lax.psum(local_dot(residual, residual), 'dom')  506 us
    psum x7, blocking collectives, shards(): alpha = norm_now / lax.psum(local_dot(direction, image), 'dom')  470 us
    psum x1, blocking collectives, shards(): rve_totals = lax.psum(partial_here, 'dom')  62.7 us
    reduce_sum x15, other arithmetic, local_dot(): return jnp.sum(first * second, axis=(1, 2, 3))  61.2 us
    ppermute x9, starting transfers between devices, padded_2(): before = lax.ppermute(last, axis, up)  29 us
  transfers between devices with their start and end apart: 18, of which 6 were waited for; matrix products, arithmetic and copies ran while one was open for 1% of the time, Pallas kernels for 0%

commit v1 on v0

--- a/solution.py
+++ b/solution.py
@@ -23,6 +23,63 @@
         after = lax.ppermute(leading, axis, down)
         value = jnp.concatenate([before, value, after], axis=dim)
     return value
+
+
+def xor_groups(size):
+    bits = size.bit_length() - 1
+    if size != 1 << bits:
+        return None
+    groups = [(0, 1)] if bits % 2 else []
+    lo = bits % 2
+    while lo < bits:
+        groups.append((lo, 2))
+        lo += 2
+    return groups
+
+
+def tree_sum(vals, nb):
+    cur = dict(vals)
+    for level in range(nb):
+        cur = {o: v + cur[o | (1 << level)] for o, v in cur.items() if not o & (1 << level)}
+    return cur[0]
+
+
+def axis_sum(value, axis):
+    size = lax.axis_size(axis)
+    groups = xor_groups(size)
+    if groups is None:
+        return lax.psum(value, axis)
+    for lo, nb in groups:
+        vals = {0: value}
+        for o in range(1, 1 << nb):
+            mask = o << lo
+            vals[o] = lax.ppermute(value, axis, [(i, i ^ mask) for i in range(size)])
+        value = tree_sum(vals, nb)
+    return value
+
+
+def axis_gather(value, axis):
+    size = lax.axis_size(axis)
+    if xor_groups(size) is None:
+        return [lax.all_gather(value, axis, axis=0, tiled=True)], None
+    parts = [value] + [
+        lax.ppermute(value, axis, [(i, i ^ o) for i in range(size)]) for o in range(1, size)
+    ]
+    return parts, lax.axis_index(axis)
+
+
+def axis_reduce_scatter(value, axis):
+    size = lax.axis_size(axis)
+    if xor_groups(size) is None:
+        return lax.psum_scatter(value, axis, scatter_dimension=0, tiled=True)
+    me = lax.axis_index(axis)
+    block = value.shape[0] // size
+    nb = size.bit_length() - 1
+    vals = {0: lax.dynamic_slice_in_dim(value, me * block, block, 0)}
+    for o in range(1, size):
+        wanted = lax.dynamic_slice_in_dim(value, (me ^ o) * block, block, 0)
+        vals[o] = lax.ppermute(wanted, axis, [(i, i ^ o) for i in range(size)])
+    return tree_sum(vals, nb)
 
 
 def shift_cells(field, step):
@@ -59,8 +116,20 @@
             softening = softening + active * looked[1 + slip]
         return (looked[0] / (1.0 + softening)).reshape(codes.shape)
 
-    all_strains = lax.all_gather(macro_adjoint, "hot", axis=0, tiled=True)
     spot_onehot = (rve_spot[:, None] == jnp.arange(spot_count)[None, :]).astype(jnp.float32)
+    parts, hot_me = axis_gather(macro_adjoint, "hot")
+    if hot_me is None:
+        all_strains = parts[0]
+    else:
+        local = macro_adjoint.shape[0]
+        ordered = []
+        for j in range(len(parts)):
+            pick = [(hot_me ^ o) == j for o in range(len(parts))]
+            block = parts[0]
+            for o in range(1, len(parts)):
+                block = jnp.where(pick[o], parts[o], block)
+            ordered.append(block)
+        all_strains = jnp.concatenate(ordered, 0)
     strains = jnp.dot(
         spot_onehot,
         all_strains,
@@ -71,7 +140,7 @@
     padded = padded_2(stiff, (("dom", 1),), 1)
 
     def squares(residual):
-        return lax.psum(local_dot(residual, residual), "dom")
+        return axis_sum(local_dot(residual, residual), "dom")
 
     near_xup = padded[:, 2:]
     near_xdn = padded[:, :-2]
@@ -115,8 +184,8 @@
     residual = source
     direction = source
     norm_now = squares(residual)
+    wide = padded_2(direction, (("dom", 2),), 1)
     for step in range(ITERS):
-        wide = padded_2(direction, (("dom", 2),), 1)
         image = (
             diagonal_sum * direction
             - face_xup[:, None] * wide[:, :, 2:]
@@ -126,11 +195,19 @@
             - face_zup[:, None] * (shift_cells(direction, 1) * upper_mask)
             - face_zdn[:, None] * (shift_cells(direction, -1) * lower_mask)
         )
-        alpha = norm_now / lax.psum(local_dot(direction, image), "dom")
+        alpha = norm_now / axis_sum(local_dot(direction, image), "dom")
         answer = answer + expand(alpha) * direction
         residual = residual - expand(alpha) * image
         norm_next = squares(residual)
-        direction = residual + expand(norm_next / norm_now) * direction
+        beta = expand(norm_next / norm_now)
+        if step + 1 < ITERS:
+            wide_residual = padded_2(residual, (("dom", 2),), 1)
+            edges = jnp.concatenate([wide[:, :, :1], wide[:, :, -1:]], 2)
+            edges_residual = jnp.concatenate([wide_residual[:, :, :1], wide_residual[:, :, -1:]], 2)
+            edges = edges_residual + beta * edges
+        direction = residual + beta * direction
+        if step + 1 < ITERS:
+            wide = jnp.concatenate([edges[:, :, :1], direction, edges[:, :, 1:]], 2)
         norm_now = norm_next
     volume = float(RES**3)
     stiff_part = jnp.sum(stiff, axis=(1, 2)) / volume
@@ -150,14 +227,14 @@
         1,
     )
     per_spot = float(rve_count * lax.axis_size("hot") // spot_count)
-    rve_totals = lax.psum(partial_here, "dom")
+    rve_totals = axis_sum(partial_here, "dom")
     spot_local = jnp.dot(
         spot_onehot.T,
         rve_totals,
         precision=lax.Precision.HIGHEST,
         preferred_element_type=jnp.float32,
     )
-    owned = lax.psum_scatter(spot_local, "hot", scatter_dimension=0, tiled=True)
+    owned = axis_reduce_scatter(spot_local, "hot")
     return (owned / per_spot, answer)
 
 

time: 1260 us -> 474 us (0.38)
  blocking collectives: 1060 us -> 0 us
  starting transfers between devices: 40.6 us -> 203 us
  waiting for transfers between devices: 2.06 us -> 125 us
  other arithmetic: 101 us -> 80.9 us
    psum x16 -> x0, blocking collectives: 1040 us -> none  [the longest x8 506 us: squares(): return lax.psum(local_dot(residual, residual), 'dom')]
    ppermute x0 -> x125, starting transfers between devices: none -> 167 us  [the longest x119 158 us: axis_sum(): vals[o] = lax.ppermute(value, axis, [(i, i ^ mask) for i in range(size)])]
    ppermute x0 -> x125, waiting for transfers between devices: none -> 125 us  [the longest x119 120 us: axis_sum(): vals[o] = lax.ppermute(value, axis, [(i, i ^ mask) for i in range(size)])]
    reduce_sum x15, other arithmetic: 61.2 us -> 43.4 us  [local_dot(): return jnp.sum(first * second, axis=(1, 2, 3))]
  transfers between devices with their start and end apart: 18 -> 143, of which waited for: 6 -> 84; matrix products, arithmetic and copies ran while one was open for 1% -> 11% of each run, Pallas kernels for 0% -> 0%
where the time goes in v1:
time: 474 us; the launch traced here: 464 us
  starting transfers between devices  203 us (43%)
  waiting for transfers between devices  125 us (26%)
  other arithmetic  80.9 us (17%)
  local copies, waits for them, and re-layouts  46.4 us (10%)
  matrix products  6.38 us (1%)
    ppermute x119, starting transfers between devices, axis_sum(): vals[o] = lax.ppermute(value, axis, [(i, i ^ mask) for i in range(size)])  158 us
    ppermute x119, waiting for transfers between devices, axis_sum(): vals[o] = lax.ppermute(value, axis, [(i, i ^ mask) for i in range(size)])  120 us
    reduce_sum x15, other arithmetic, local_dot(): return jnp.sum(first * second, axis=(1, 2, 3))  43.4 us
    ppermute x9, starting transfers between devices, padded_2(): before = lax.ppermute(last, axis, up)  24.5 us
    dynamic_update_slice x8, other arithmetic, shards(): stiff = lax.map(stiff_one, (slip_code, grain_id))  16.6 us
    slice x18, local copies, waits for them, and re-layouts, shift_cells(): return jnp.concatenate([field[..., step:], filler], -1)  15 us
    ppermute x9, starting transfers between devices, padded_2(): after = lax.ppermute(leading, axis, down)  11.6 us
    add x6, other arithmetic, shards(): edges = edges_residual + beta * edges  11.2 us
  transfers between devices with their start and end apart: 143, of which 84 were waited for; matrix products, arithmetic and copies ran while one was open for 11% of the time, Pallas kernels for 0%

profile of v1, /device:TPU:0, one launch (start us, length us, event | category | flops | bytes accessed | tf_op | source)
XLA Modules:
  0.0 464.4 jit_solution(13985146824423943770)
XLA Ops:
  0.6 4.1 collective-permute-start.1
  6.4 40.5 %while.13 = (s32[]{:T(128)}, f32[8,2,4096]{2,1,0:T(2,128)S(1)}, s32[8,2,4096]{2,1,0:T(2,128)}, f32[13,64]{1,0:T(8,128)S(1)}, s32[8,2,4096]{2,1,0:T(2,128)}, /*index=5*/s32[]{:T(128)}) while((s32[]{:T(128)}, f32[8,2,4096]{2,1,0:T(2,128)S(1)}, s32[8,2,4096]{2,1,0:T(2,128)}, f32[13,64]{1,0:T(8,128)S(1)}, s32[8,2,4096]{2,1,0:T(2,128)}, ...), condition=%wide.region_1.2_spmd, body=%wide.region_0.1_spmd.sunk | while | flops 84582400 | bytes 2788693 | solution.py:139
  48.4 3.0 collective-permute-start.4
  58.7 4.5 collective-permute-start.13
  64.5 5.1 %multiply_reduce_fusion.14 = (f32[8]{0:T(128)S(1)}, f32[8]{0:T(128)S(1)}, f32[8,3,2,4096]{3,2,0,1:T(2,128)S(1)}) fusion(f32[4096]{0:T(1024)S(1)} %get-tuple-element.321, f32[8,3,2,4095]{3,2,0,1:T(2,128)S(1)} %get-tuple-element.280, f32[8,2,4096]{2,1,0:T(2,128)S(1)} %get-tuple-element.210, f32[4096]{0:T(1024)S(1)} %get-tuple-element.320, ...), kind=kLoop, calls=%fused_computation.253 | loop fusion | flops 5308400 | bytes 7347904 | tf_op jit(solution)/shard_map/reduce_sum | solution.py:93
  69.6 5.6 %collective-permute-start.14 = (f32[8]{0:T(128)S(1)}, f32[8]{0:T(128)S(1)}, u32[]{:S(2)}, u32[]{:S(2)}) collective-permute-start(f32[8]{0:T(128)S(1)} %get-tuple-element.149), channel_id=1, source_target_pairs={{0,1},{1,0},{2,3},{3,2},{4,5},{5,4},{6,7},{7,6},{8,9},{9,8},{10,11... | collective-permute-start | bytes 104 | tf_op jit(solution)/shard_map/ppermute | solution.py:56
  76.1 6.4 %collective-permute-start.17 = (f32[8]{0:T(128)S(1)}, f32[8]{0:T(128)S(1)}, u32[]{:S(2)}, u32[]{:S(2)}) collective-permute-start(f32[8]{0:T(128)S(1)} %add.1001), channel_id=1, source_target_pairs={{0,6},{1,7},{2,4},{3,5},{4,2},{5,3},{6,0},{7,1},{8,14},{9,15},{10,... | collective-permute-start | bytes 104 | tf_op jit(solution)/shard_map/ppermute | solution.py:56
  83.3 3.2 collective-permute-start.8
  87.5 7.1 %collective-permute-start.20 = (f32[8]{0:T(128)S(1)}, f32[8]{0:T(128)S(1)}, u32[]{:S(2)}, u32[]{:S(2)}) collective-permute-start(f32[8]{0:T(128)S(1)} %add_add_fusion.23), channel_id=1, source_target_pairs={{0,24},{1,25},{2,26},{3,27},{4,28},{5,29},{6,30},{7,31},{8,16},{9,... | collective-permute-start | bytes 104 | tf_op jit(solution)/shard_map/ppermute | solution.py:56
  95.6 3.2 collective-permute-start.11
  100.4 3.4 collective-permute-done.10
  117.5 2.7 collective-permute-start.27
  122.3 3.0 collective-permute-done.26
  130.0 4.6 multiply_reduce_fusion.12
  135.7 3.3 collective-permute-start.33
  140.6 3.5 collective-permute-done.32
  144.1 2.6 collective-permute-start.36
  149.0 2.8 collective-permute-done.35
  157.4 2.8 collective-permute-start.40
  162.2 3.0 collective-permute-done.39
  165.4 2.7 collective-permute-start.43
  170.1 3.0 collective-permute-done.42
  177.7 4.6 multiply_reduce_fusion.10
  183.5 3.3 collective-permute-start.49
  188.3 3.5 collective-permute-done.48
  196.7 2.6 collective-permute-done.51
  204.9 2.8 collective-permute-start.56
  209.8 3.0 collective-permute-done.55
  212.9 2.7 collective-permute-start.59
  217.7 3.0 collective-permute-done.58
  225.3 4.6 multiply_reduce_fusion.8
  231.0 3.3 collective-permute-start.65
  235.9 3.5 collective-permute-done.64
  244.3 2.6 collective-permute-done.67
  252.5 2.8 collective-permute-start.72
  257.3 3.0 collective-permute-done.71
  260.4 2.7 collective-permute-start.75
  265.2 3.0 collective-permute-done.74
  273.1 4.6 multiply_reduce_fusion.6
  278.8 3.3 collective-permute-start.81
  283.7 3.5 collective-permute-done.80
  300.2 2.8 collective-permute-start.88
  305.1 3.0 collective-permute-done.87
  308.2 2.7 collective-permute-start.91
  313.0 3.0 collective-permute-done.90
  320.6 4.6 multiply_reduce_fusion.4
  326.3 3.3 collective-permute-start.97
  331.2 3.5 collective-permute-done.96
  347.8 2.8 collective-permute-start.104
  352.6 3.0 collective-permute-done.103
  355.7 2.7 collective-permute-start.107
  360.5 3.0 collective-permute-done.106
  368.1 4.6 multiply_reduce_fusion.2
  373.9 3.3 collective-permute-start.113
  378.8 3.5 collective-permute-done.112
  395.3 2.8 collective-permute-start.120
  400.2 3.0 collective-permute-done.119
  403.3 2.7 collective-permute-start.123
  408.1 3.0 collective-permute-done.122
  411.2 3.6 multiply_add_fusion.1
  417.5 4.3 multiply_reduce_fusion
  422.9 3.3 collective-permute-start.129
  427.8 3.5 collective-permute-done.128
  460.4 2.8 collective-permute-done.141
  (496 shorter events, 244.2 us)
Async XLA Ops:
  0.6 51.6 %collective-permute-start.1 = (f32[4,6]{1,0:T(4,128)}, f32[4,6]{1,0:T(4,128)S(1)}, u32[]{:S(2)}, u32[]{:S(2)}) collective-permute-start(f32[4,6]{1,0:T(4,128)} %param.8), channel_id=1, source_target_pairs={{0,64},{32,96},{64,0},{96,32},{1,65},{33,97},{65,1},{97,33},{2,66}... | collective-permute-start | bytes 296 | tf_op jit(solution)/shard_map/ppermute | solution.py:66
  4.7 47.6 %collective-permute-start = (f32[4,6]{1,0:T(4,128)}, f32[4,6]{1,0:T(4,128)S(1)}, u32[]{:S(2)}, u32[]{:S(2)}) collective-permute-start(f32[4,6]{1,0:T(4,128)} %param.8), channel_id=1, source_target_pairs={{0,96},{32,64},{64,32},{96,0},{1,97},{33,65},{65,33},{97,1},{2,98}... | collective-permute-start | bytes 296 | tf_op jit(solution)/shard_map/ppermute | solution.py:66
  5.4 46.9 %collective-permute-start.2 = (f32[4,6]{1,0:T(4,128)}, f32[4,6]{1,0:T(4,128)S(1)}, u32[]{:S(2)}, u32[]{:S(2)}) collective-permute-start(f32[4,6]{1,0:T(4,128)} %param.8), channel_id=1, source_target_pairs={{0,32},{32,0},{64,96},{96,64},{1,33},{33,1},{65,97},{97,65},{2,34}... | collective-permute-start | bytes 296 | tf_op jit(solution)/shard_map/ppermute | solution.py:66
  47.1 5.7 %collective-permute-start.3 = (f32[8,1,4096]{2,1,0:T(1,128)S(1)}, f32[8,1,4096]{2,1,0:T(1,128)S(1)}, u32[]{:S(2)}, u32[]{:S(2)}) collective-permute-start(f32[8,1,4096]{2,1,0:T(1,128)S(1)} %get-tuple-element.286), channel_id=1, source_target_pairs={{1,0},{2,1},{3,2},{4,3},{5,4},{6,5},{7,6},{8,7},{9,8},{10,9},{11,1... | collective-permute-start | bytes 393224 | tf_op jit(solution)/shard_map/ppermute | solution.py:23
  57.4 7.1 %collective-permute-start.12 = (f32[8,3,1,4096]{3,2,0,1:T(1,128)S(1)}, f32[8,3,1,4096]{3,2,0,1:T(1,128)S(1)}, u32[]{:S(2)}, u32[]{:S(2)}) collective-permute-start(f32[8,3,1,4096]{3,2,0,1:T(1,128)S(1)} %get-tuple-element.275), channel_id=1, source_target_pairs={{1,0},{2,1},{3,2},{4,3},{5,4},{6,5},{7,6},{8,7},{9,8},{10,9},{11,1... | collective-permute-start | bytes 1179656 | tf_op jit(solution)/shard_map/ppermute | solution.py:23
  58.7 5.8 %collective-permute-start.13 = (f32[8,3,1,4096]{3,2,0,1:T(1,128)S(1)}, f32[8,3,1,4096]{3,2,0,1:T(1,128)S(1)}, u32[]{:S(2)}, u32[]{:S(2)}) collective-permute-start(f32[8,3,1,4096]{3,2,0,1:T(1,128)S(1)} %get-tuple-element.276), channel_id=1, source_target_pairs={{0,1},{1,2},{2,3},{3,4},{4,5},{5,6},{6,7},{7,8},{8,9},{9,10},{10,1... | collective-permute-start | bytes 1179656 | tf_op jit(solution)/shard_map/ppermute | solution.py:22
  69.6 6.5 %collective-permute-start.14 = (f32[8]{0:T(128)S(1)}, f32[8]{0:T(128)S(1)}, u32[]{:S(2)}, u32[]{:S(2)}) collective-permute-start(f32[8]{0:T(128)S(1)} %get-tuple-element.149), channel_id=1, source_target_pairs={{0,1},{1,0},{2,3},{3,2},{4,5},{5,4},{6,7},{7,6},{8,9},{9,8},{10,11... | collective-permute-start | bytes 104 | tf_op jit(solution)/shard_map/ppermute | solution.py:56
  75.2 8.1 %collective-permute-start.5 = (f32[8]{0:T(128)S(1)}, f32[8]{0:T(128)S(1)}, u32[]{:S(2)}, u32[]{:S(2)}) collective-permute-start(f32[8]{0:T(128)S(1)} %get-tuple-element.150), channel_id=1, source_target_pairs={{0,1},{1,0},{2,3},{3,2},{4,5},{5,4},{6,7},{7,6},{8,9},{9,8},{10,11... | collective-permute-start | bytes 104 | tf_op jit(solution)/shard_map/ppermute | solution.py:56
  76.1 10.5 %collective-permute-start.17 = (f32[8]{0:T(128)S(1)}, f32[8]{0:T(128)S(1)}, u32[]{:S(2)}, u32[]{:S(2)}) collective-permute-start(f32[8]{0:T(128)S(1)} %add.1001), channel_id=1, source_target_pairs={{0,6},{1,7},{2,4},{3,5},{4,2},{5,3},{6,0},{7,1},{8,14},{9,15},{10,... | collective-permute-start | bytes 104 | tf_op jit(solution)/shard_map/ppermute | solution.py:56
  82.4 5.1 %collective-permute-start.16 = (f32[8]{0:T(128)S(1)}, f32[8]{0:T(128)S(1)}, u32[]{:S(2)}, u32[]{:S(2)}) collective-permute-start(f32[8]{0:T(128)S(1)} %add.1001), channel_id=1, source_target_pairs={{0,4},{1,5},{2,6},{3,7},{4,0},{5,1},{6,2},{7,3},{8,12},{9,13},{10,... | collective-permute-start | bytes 104 | tf_op jit(solution)/shard_map/ppermute | solution.py:56
  82.4 5.1 %collective-permute-start.15 = (f32[8]{0:T(128)S(1)}, f32[8]{0:T(128)S(1)}, u32[]{:S(2)}, u32[]{:S(2)}) collective-permute-start(f32[8]{0:T(128)S(1)} %add.1001), channel_id=1, source_target_pairs={{0,2},{1,3},{2,0},{3,1},{4,6},{5,7},{6,4},{7,5},{8,10},{9,11},{10,... | collective-permute-start | bytes 104 | tf_op jit(solution)/shard_map/ppermute | solution.py:56
  83.3 11.6 %collective-permute-start.8 = (f32[8]{0:T(128)S(1)}, f32[8]{0:T(128)S(1)}, u32[]{:S(2)}, u32[]{:S(2)}) collective-permute-start(f32[8]{0:T(128)S(1)} %add.981), channel_id=1, source_target_pairs={{0,6},{1,7},{2,4},{3,5},{4,2},{5,3},{6,0},{7,1},{8,14},{9,15},{10,... | collective-permute-start | bytes 104 | tf_op jit(solution)/shard_map/ppermute | solution.py:56
  86.5 9.0 %collective-permute-start.7 = (f32[8]{0:T(128)S(1)}, f32[8]{0:T(128)S(1)}, u32[]{:S(2)}, u32[]{:S(2)}) collective-permute-start(f32[8]{0:T(128)S(1)} %add.981), channel_id=1, source_target_pairs={{0,4},{1,5},{2,6},{3,7},{4,0},{5,1},{6,2},{7,3},{8,12},{9,13},{10,... | collective-permute-start | bytes 104 | tf_op jit(solution)/shard_map/ppermute | solution.py:56
  86.5 9.0 %collective-permute-start.6 = (f32[8]{0:T(128)S(1)}, f32[8]{0:T(128)S(1)}, u32[]{:S(2)}, u32[]{:S(2)}) collective-permute-start(f32[8]{0:T(128)S(1)} %add.981), channel_id=1, source_target_pairs={{0,2},{1,3},{2,0},{3,1},{4,6},{5,7},{6,4},{7,5},{8,10},{9,11},{10,... | collective-permute-start | bytes 104 | tf_op jit(solution)/shard_map/ppermute | solution.py:56
  87.5 11.6 %collective-permute-start.20 = (f32[8]{0:T(128)S(1)}, f32[8]{0:T(128)S(1)}, u32[]{:S(2)}, u32[]{:S(2)}) collective-permute-start(f32[8]{0:T(128)S(1)} %add_add_fusion.23), channel_id=1, source_target_pairs={{0,24},{1,25},{2,26},{3,27},{4,28},{5,29},{6,30},{7,31},{8,16},{9,... | collective-permute-start | bytes 104 | tf_op jit(solution)/shard_map/ppermute | solution.py:56
  94.6 5.2 %collective-permute-start.19 = (f32[8]{0:T(128)S(1)}, f32[8]{0:T(128)S(1)}, u32[]{:S(2)}, u32[]{:S(2)}) collective-permute-start(f32[8]{0:T(128)S(1)} %add_add_fusion.23), channel_id=1, source_target_pairs={{0,16},{1,17},{2,18},{3,19},{4,20},{5,21},{6,22},{7,23},{8,24},{9,... | collective-permute-start | bytes 104 | tf_op jit(solution)/shard_map/ppermute | solution.py:56
  98.8 5.1 %collective-permute-start.10 = (f32[8]{0:T(128)S(1)}, f32[8]{0:T(128)S(1)}, u32[]{:S(2)}, u32[]{:S(2)}) collective-permute-start(f32[8]{0:T(128)S(1)} %add_add_fusion.25), channel_id=1, source_target_pairs={{0,16},{1,17},{2,18},{3,19},{4,20},{5,21},{6,22},{7,23},{8,24},{9,... | collective-permute-start | bytes 104 | tf_op jit(solution)/shard_map/ppermute | solution.py:56
  105.8 19.5 %collective-permute-start.28 = (f32[8,3,1,4096]{3,2,0,1:T(1,128)S(1)}, f32[8,3,1,4096]{3,2,0,1:T(1,128)S(1)}, u32[]{:S(2)}, u32[]{:S(2)}) collective-permute-start(f32[8,3,1,4096]{3,2,0,1:T(1,128)S(1)} %get-tuple-element.269), channel_id=1, source_target_pairs={{0,1},{1,2},{2,3},{3,4},{4,5},{5,6},{6,7},{7,8},{8,9},{9,10},{10,1... | collective-permute-start | bytes 1179656 | tf_op jit(solution)/shard_map/ppermute | solution.py:22
  108.2 17.1 %collective-permute-start.29 = (f32[8,3,1,4096]{3,2,0,1:T(1,128)S(1)}, f32[8,3,1,4096]{3,2,0,1:T(1,128)S(1)}, u32[]{:S(2)}, u32[]{:S(2)}) collective-permute-start(f32[8,3,1,4096]{3,2,0,1:T(1,128)S(1)} %get-tuple-element.270), channel_id=1, source_target_pairs={{1,0},{2,1},{3,2},{4,3},{5,4},{6,5},{7,6},{8,7},{9,8},{10,9},{11,1... | collective-permute-start | bytes 1179656 | tf_op jit(solution)/shard_map/ppermute | solution.py:23
  111.6 5.1 %collective-permute-start.23 = (f32[8]{0:T(128)S(1)}, f32[8]{0:T(128)S(1)}, u32[]{:S(2)}, u32[]{:S(2)}) collective-permute-start(f32[8]{0:T(128)S(1)} %add.1008), channel_id=1, source_target_pairs={{0,4},{1,5},{2,6},{3,7},{4,0},{5,1},{6,2},{7,3},{8,12},{9,13},{10,... | collective-permute-start | bytes 104 | tf_op jit(solution)/shard_map/ppermute | solution.py:56
  120.3 5.1 %collective-permute-start.26 = (f32[8]{0:T(128)S(1)}, f32[8]{0:T(128)S(1)}, u32[]{:S(2)}, u32[]{:S(2)}) collective-permute-start(f32[8]{0:T(128)S(1)} %add_add_fusion.22), channel_id=1, source_target_pairs={{0,16},{1,17},{2,18},{3,19},{4,20},{5,21},{6,22},{7,23},{8,24},{9,... | collective-permute-start | bytes 104 | tf_op jit(solution)/shard_map/ppermute | solution.py:56
  139.0 5.1 %collective-permute-start.32 = (f32[8]{0:T(128)S(1)}, f32[8]{0:T(128)S(1)}, u32[]{:S(2)}, u32[]{:S(2)}) collective-permute-start(f32[8]{0:T(128)S(1)} %add.1017), channel_id=1, source_target_pairs={{0,4},{1,5},{2,6},{3,7},{4,0},{5,1},{6,2},{7,3},{8,12},{9,13},{10,... | collective-permute-start | bytes 104 | tf_op jit(solution)/shard_map/ppermute | solution.py:56
  146.7 5.1 %collective-permute-start.35 = (f32[8]{0:T(128)S(1)}, f32[8]{0:T(128)S(1)}, u32[]{:S(2)}, u32[]{:S(2)}) collective-permute-start(f32[8]{0:T(128)S(1)} %add_add_fusion.20), channel_id=1, source_target_pairs={{0,16},{1,17},{2,18},{3,19},{4,20},{5,21},{6,22},{7,23},{8,24},{9,... | collective-permute-start | bytes 104 | tf_op jit(solution)/shard_map/ppermute | solution.py:56
  153.6 19.5 %collective-permute-start.44 = (f32[8,3,1,4096]{3,2,0,1:T(1,128)S(1)}, f32[8,3,1,4096]{3,2,0,1:T(1,128)S(1)}, u32[]{:S(2)}, u32[]{:S(2)}) collective-permute-start(f32[8,3,1,4096]{3,2,0,1:T(1,128)S(1)} %get-tuple-element.261), channel_id=1, source_target_pairs={{0,1},{1,2},{2,3},{3,4},{4,5},{5,6},{6,7},{7,8},{8,9},{9,10},{10,1... | collective-permute-start | bytes 1179656 | tf_op jit(solution)/shard_map/ppermute | solution.py:22
  156.1 17.1 %collective-permute-start.45 = (f32[8,3,1,4096]{3,2,0,1:T(1,128)S(1)}, f32[8,3,1,4096]{3,2,0,1:T(1,128)S(1)}, u32[]{:S(2)}, u32[]{:S(2)}) collective-permute-start(f32[8,3,1,4096]{3,2,0,1:T(1,128)S(1)} %get-tuple-element.262), channel_id=1, source_target_pairs={{1,0},{2,1},{3,2},{4,3},{5,4},{6,5},{7,6},{8,7},{9,8},{10,9},{11,1... | collective-permute-start | bytes 1179656 | tf_op jit(solution)/shard_map/ppermute | solution.py:23
  160.2 5.1 %collective-permute-start.39 = (f32[8]{0:T(128)S(1)}, f32[8]{0:T(128)S(1)}, u32[]{:S(2)}, u32[]{:S(2)}) collective-permute-start(f32[8]{0:T(128)S(1)} %add.1025), channel_id=1, source_target_pairs={{0,4},{1,5},{2,6},{3,7},{4,0},{5,1},{6,2},{7,3},{8,12},{9,13},{10,... | collective-permute-start | bytes 104 | tf_op jit(solution)/shard_map/ppermute | solution.py:56
  168.1 5.1 %collective-permute-start.42 = (f32[8]{0:T(128)S(1)}, f32[8]{0:T(128)S(1)}, u32[]{:S(2)}, u32[]{:S(2)}) collective-permute-start(f32[8]{0:T(128)S(1)} %add_add_fusion.19), channel_id=1, source_target_pairs={{0,16},{1,17},{2,18},{3,19},{4,20},{5,21},{6,22},{7,23},{8,24},{9,... | collective-permute-start | bytes 104 | tf_op jit(solution)/shard_map/ppermute | solution.py:56
  186.8 5.1 %collective-permute-start.48 = (f32[8]{0:T(128)S(1)}, f32[8]{0:T(128)S(1)}, u32[]{:S(2)}, u32[]{:S(2)}) collective-permute-start(f32[8]{0:T(128)S(1)} %add.1034), channel_id=1, source_target_pairs={{0,4},{1,5},{2,6},{3,7},{4,0},{5,1},{6,2},{7,3},{8,12},{9,13},{10,... | collective-permute-start | bytes 104 | tf_op jit(solution)/shard_map/ppermute | solution.py:56
  194.2 5.1 %collective-permute-start.51 = (f32[8]{0:T(128)S(1)}, f32[8]{0:T(128)S(1)}, u32[]{:S(2)}, u32[]{:S(2)}) collective-permute-start(f32[8]{0:T(128)S(1)} %add_add_fusion.17), channel_id=1, source_target_pairs={{0,16},{1,17},{2,18},{3,19},{4,20},{5,21},{6,22},{7,23},{8,24},{9,... | collective-permute-start | bytes 104 | tf_op jit(solution)/shard_map/ppermute | solution.py:56
  201.1 19.6 %collective-permute-start.60 = (f32[8,3,1,4096]{3,2,0,1:T(1,128)S(1)}, f32[8,3,1,4096]{3,2,0,1:T(1,128)S(1)}, u32[]{:S(2)}, u32[]{:S(2)}) collective-permute-start(f32[8,3,1,4096]{3,2,0,1:T(1,128)S(1)} %get-tuple-element.253), channel_id=1, source_target_pairs={{0,1},{1,2},{2,3},{3,4},{4,5},{5,6},{6,7},{7,8},{8,9},{9,10},{10,1... | collective-permute-start | bytes 1179656 | tf_op jit(solution)/shard_map/ppermute | solution.py:22
  203.6 17.2 %collective-permute-start.61 = (f32[8,3,1,4096]{3,2,0,1:T(1,128)S(1)}, f32[8,3,1,4096]{3,2,0,1:T(1,128)S(1)}, u32[]{:S(2)}, u32[]{:S(2)}) collective-permute-start(f32[8,3,1,4096]{3,2,0,1:T(1,128)S(1)} %get-tuple-element.254), channel_id=1, source_target_pairs={{1,0},{2,1},{3,2},{4,3},{5,4},{6,5},{7,6},{8,7},{9,8},{10,9},{11,1... | collective-permute-start | bytes 1179656 | tf_op jit(solution)/shard_map/ppermute | solution.py:23
  207.7 5.1 %collective-permute-start.55 = (f32[8]{0:T(128)S(1)}, f32[8]{0:T(128)S(1)}, u32[]{:S(2)}, u32[]{:S(2)}) collective-permute-start(f32[8]{0:T(128)S(1)} %add.1042), channel_id=1, source_target_pairs={{0,4},{1,5},{2,6},{3,7},{4,0},{5,1},{6,2},{7,3},{8,12},{9,13},{10,... | collective-permute-start | bytes 104 | tf_op jit(solution)/shard_map/ppermute | solution.py:56
  215.6 5.1 %collective-permute-start.58 = (f32[8]{0:T(128)S(1)}, f32[8]{0:T(128)S(1)}, u32[]{:S(2)}, u32[]{:S(2)}) collective-permute-start(f32[8]{0:T(128)S(1)} %add_add_fusion.16), channel_id=1, source_target_pairs={{0,16},{1,17},{2,18},{3,19},{4,20},{5,21},{6,22},{7,23},{8,24},{9,... | collective-permute-start | bytes 104 | tf_op jit(solution)/shard_map/ppermute | solution.py:56
  234.4 5.1 %collective-permute-start.64 = (f32[8]{0:T(128)S(1)}, f32[8]{0:T(128)S(1)}, u32[]{:S(2)}, u32[]{:S(2)}) collective-permute-start(f32[8]{0:T(128)S(1)} %add.1051), channel_id=1, source_target_pairs={{0,4},{1,5},{2,6},{3,7},{4,0},{5,1},{6,2},{7,3},{8,12},{9,13},{10,... | collective-permute-start | bytes 104 | tf_op jit(solution)/shard_map/ppermute | solution.py:56
  241.8 5.1 %collective-permute-start.67 = (f32[8]{0:T(128)S(1)}, f32[8]{0:T(128)S(1)}, u32[]{:S(2)}, u32[]{:S(2)}) collective-permute-start(f32[8]{0:T(128)S(1)} %add_add_fusion.14), channel_id=1, source_target_pairs={{0,16},{1,17},{2,18},{3,19},{4,20},{5,21},{6,22},{7,23},{8,24},{9,... | collective-permute-start | bytes 104 | tf_op jit(solution)/shard_map/ppermute | solution.py:56
  248.7 19.8 %collective-permute-start.76 = (f32[8,3,1,4096]{3,2,0,1:T(1,128)S(1)}, f32[8,3,1,4096]{3,2,0,1:T(1,128)S(1)}, u32[]{:S(2)}, u32[]{:S(2)}) collective-permute-start(f32[8,3,1,4096]{3,2,0,1:T(1,128)S(1)} %get-tuple-element.245), channel_id=1, source_target_pairs={{0,1},{1,2},{2,3},{3,4},{4,5},{5,6},{6,7},{7,8},{8,9},{9,10},{10,1... | collective-permute-start | bytes 1179656 | tf_op jit(solution)/shard_map/ppermute | solution.py:22
  251.1 17.4 %collective-permute-start.77 = (f32[8,3,1,4096]{3,2,0,1:T(1,128)S(1)}, f32[8,3,1,4096]{3,2,0,1:T(1,128)S(1)}, u32[]{:S(2)}, u32[]{:S(2)}) collective-permute-start(f32[8,3,1,4096]{3,2,0,1:T(1,128)S(1)} %get-tuple-element.246), channel_id=1, source_target_pairs={{1,0},{2,1},{3,2},{4,3},{5,4},{6,5},{7,6},{8,7},{9,8},{10,9},{11,1... | collective-permute-start | bytes 1179656 | tf_op jit(solution)/shard_map/ppermute | solution.py:23
  255.3 5.1 %collective-permute-start.71 = (f32[8]{0:T(128)S(1)}, f32[8]{0:T(128)S(1)}, u32[]{:S(2)}, u32[]{:S(2)}) collective-permute-start(f32[8]{0:T(128)S(1)} %add.1059), channel_id=1, source_target_pairs={{0,4},{1,5},{2,6},{3,7},{4,0},{5,1},{6,2},{7,3},{8,12},{9,13},{10,... | collective-permute-start | bytes 104 | tf_op jit(solution)/shard_map/ppermute | solution.py:56
  263.2 5.1 %collective-permute-start.74 = (f32[8]{0:T(128)S(1)}, f32[8]{0:T(128)S(1)}, u32[]{:S(2)}, u32[]{:S(2)}) collective-permute-start(f32[8]{0:T(128)S(1)} %add_add_fusion.13), channel_id=1, source_target_pairs={{0,16},{1,17},{2,18},{3,19},{4,20},{5,21},{6,22},{7,23},{8,24},{9,... | collective-permute-start | bytes 104 | tf_op jit(solution)/shard_map/ppermute | solution.py:56
  278.8 4.9 %collective-permute-start.81 = (f32[8]{0:T(128)S(1)}, f32[8]{0:T(128)S(1)}, u32[]{:S(2)}, u32[]{:S(2)}) collective-permute-start(f32[8]{0:T(128)S(1)} %add.1068), channel_id=1, source_target_pairs={{0,6},{1,7},{2,4},{3,5},{4,2},{5,3},{6,0},{7,1},{8,14},{9,15},{10,... | collective-permute-start | bytes 104 | tf_op jit(solution)/shard_map/ppermute | solution.py:56
  282.1 5.1 %collective-permute-start.80 = (f32[8]{0:T(128)S(1)}, f32[8]{0:T(128)S(1)}, u32[]{:S(2)}, u32[]{:S(2)}) collective-permute-start(f32[8]{0:T(128)S(1)} %add.1068), channel_id=1, source_target_pairs={{0,4},{1,5},{2,6},{3,7},{4,0},{5,1},{6,2},{7,3},{8,12},{9,13},{10,... | collective-permute-start | bytes 104 | tf_op jit(solution)/shard_map/ppermute | solution.py:56
  289.6 5.1 %collective-permute-start.83 = (f32[8]{0:T(128)S(1)}, f32[8]{0:T(128)S(1)}, u32[]{:S(2)}, u32[]{:S(2)}) collective-permute-start(f32[8]{0:T(128)S(1)} %add_add_fusion.11), channel_id=1, source_target_pairs={{0,16},{1,17},{2,18},{3,19},{4,20},{5,21},{6,22},{7,23},{8,24},{9,... | collective-permute-start | bytes 104 | tf_op jit(solution)/shard_map/ppermute | solution.py:56
  296.5 19.6 %collective-permute-start.92 = (f32[8,3,1,4096]{3,2,0,1:T(1,128)S(1)}, f32[8,3,1,4096]{3,2,0,1:T(1,128)S(1)}, u32[]{:S(2)}, u32[]{:S(2)}) collective-permute-start(f32[8,3,1,4096]{3,2,0,1:T(1,128)S(1)} %get-tuple-element.237), channel_id=1, source_target_pairs={{0,1},{1,2},{2,3},{3,4},{4,5},{5,6},{6,7},{7,8},{8,9},{9,10},{10,1... | collective-permute-start | bytes 1179656 | tf_op jit(solution)/shard_map/ppermute | solution.py:22
  298.9 17.1 %collective-permute-start.93 = (f32[8,3,1,4096]{3,2,0,1:T(1,128)S(1)}, f32[8,3,1,4096]{3,2,0,1:T(1,128)S(1)}, u32[]{:S(2)}, u32[]{:S(2)}) collective-permute-start(f32[8,3,1,4096]{3,2,0,1:T(1,128)S(1)} %get-tuple-element.238), channel_id=1, source_target_pairs={{1,0},{2,1},{3,2},{4,3},{5,4},{6,5},{7,6},{8,7},{9,8},{10,9},{11,1... | collective-permute-start | bytes 1179656 | tf_op jit(solution)/shard_map/ppermute | solution.py:23
  303.0 5.1 %collective-permute-start.87 = (f32[8]{0:T(128)S(1)}, f32[8]{0:T(128)S(1)}, u32[]{:S(2)}, u32[]{:S(2)}) collective-permute-start(f32[8]{0:T(128)S(1)} %add.1076), channel_id=1, source_target_pairs={{0,4},{1,5},{2,6},{3,7},{4,0},{5,1},{6,2},{7,3},{8,12},{9,13},{10,... | collective-permute-start | bytes 104 | tf_op jit(solution)/shard_map/ppermute | solution.py:56
  310.9 5.1 %collective-permute-start.90 = (f32[8]{0:T(128)S(1)}, f32[8]{0:T(128)S(1)}, u32[]{:S(2)}, u32[]{:S(2)}) collective-permute-start(f32[8]{0:T(128)S(1)} %add_add_fusion.10), channel_id=1, source_target_pairs={{0,16},{1,17},{2,18},{3,19},{4,20},{5,21},{6,22},{7,23},{8,24},{9,... | collective-permute-start | bytes 104 | tf_op jit(solution)/shard_map/ppermute | solution.py:56
  326.3 4.9 %collective-permute-start.97 = (f32[8]{0:T(128)S(1)}, f32[8]{0:T(128)S(1)}, u32[]{:S(2)}, u32[]{:S(2)}) collective-permute-start(f32[8]{0:T(128)S(1)} %add.1085), channel_id=1, source_target_pairs={{0,6},{1,7},{2,4},{3,5},{4,2},{5,3},{6,0},{7,1},{8,14},{9,15},{10,... | collective-permute-start | bytes 104 | tf_op jit(solution)/shard_map/ppermute | solution.py:56
  329.7 5.1 %collective-permute-start.96 = (f32[8]{0:T(128)S(1)}, f32[8]{0:T(128)S(1)}, u32[]{:S(2)}, u32[]{:S(2)}) collective-permute-start(f32[8]{0:T(128)S(1)} %add.1085), channel_id=1, source_target_pairs={{0,4},{1,5},{2,6},{3,7},{4,0},{5,1},{6,2},{7,3},{8,12},{9,13},{10,... | collective-permute-start | bytes 104 | tf_op jit(solution)/shard_map/ppermute | solution.py:56
  337.1 5.1 %collective-permute-start.99 = (f32[8]{0:T(128)S(1)}, f32[8]{0:T(128)S(1)}, u32[]{:S(2)}, u32[]{:S(2)}) collective-permute-start(f32[8]{0:T(128)S(1)} %add_add_fusion.8), channel_id=1, source_target_pairs={{0,16},{1,17},{2,18},{3,19},{4,20},{5,21},{6,22},{7,23},{8,24},{9,... | collective-permute-start | bytes 104 | tf_op jit(solution)/shard_map/ppermute | solution.py:56
  344.0 19.6 %collective-permute-start.108 = (f32[8,3,1,4096]{3,2,0,1:T(1,128)S(1)}, f32[8,3,1,4096]{3,2,0,1:T(1,128)S(1)}, u32[]{:S(2)}, u32[]{:S(2)}) collective-permute-start(f32[8,3,1,4096]{3,2,0,1:T(1,128)S(1)} %get-tuple-element.229), channel_id=1, source_target_pairs={{0,1},{1,2},{2,3},{3,4},{4,5},{5,6},{6,7},{7,8},{8,9},{9,10},{10,1... | collective-permute-start | bytes 1179656 | tf_op jit(solution)/shard_map/ppermute | solution.py:22
  346.4 17.2 %collective-permute-start.109 = (f32[8,3,1,4096]{3,2,0,1:T(1,128)S(1)}, f32[8,3,1,4096]{3,2,0,1:T(1,128)S(1)}, u32[]{:S(2)}, u32[]{:S(2)}) collective-permute-start(f32[8,3,1,4096]{3,2,0,1:T(1,128)S(1)} %get-tuple-element.230), channel_id=1, source_target_pairs={{1,0},{2,1},{3,2},{4,3},{5,4},{6,5},{7,6},{8,7},{9,8},{10,9},{11,1... | collective-permute-start | bytes 1179656 | tf_op jit(solution)/shard_map/ppermute | solution.py:23
  350.6 5.1 %collective-permute-start.103 = (f32[8]{0:T(128)S(1)}, f32[8]{0:T(128)S(1)}, u32[]{:S(2)}, u32[]{:S(2)}) collective-permute-start(f32[8]{0:T(128)S(1)} %add.1093), channel_id=1, source_target_pairs={{0,4},{1,5},{2,6},{3,7},{4,0},{5,1},{6,2},{7,3},{8,12},{9,13},{10,... | collective-permute-start | bytes 104 | tf_op jit(solution)/shard_map/ppermute | solution.py:56
  358.5 5.1 %collective-permute-start.106 = (f32[8]{0:T(128)S(1)}, f32[8]{0:T(128)S(1)}, u32[]{:S(2)}, u32[]{:S(2)}) collective-permute-start(f32[8]{0:T(128)S(1)} %add_add_fusion.7), channel_id=1, source_target_pairs={{0,16},{1,17},{2,18},{3,19},{4,20},{5,21},{6,22},{7,23},{8,24},{9,... | collective-permute-start | bytes 104 | tf_op jit(solution)/shard_map/ppermute | solution.py:56
  377.2 5.1 %collective-permute-start.112 = (f32[8]{0:T(128)S(1)}, f32[8]{0:T(128)S(1)}, u32[]{:S(2)}, u32[]{:S(2)}) collective-permute-start(f32[8]{0:T(128)S(1)} %add.1102), channel_id=1, source_target_pairs={{0,4},{1,5},{2,6},{3,7},{4,0},{5,1},{6,2},{7,3},{8,12},{9,13},{10,... | collective-permute-start | bytes 104 | tf_op jit(solution)/shard_map/ppermute | solution.py:56
  384.7 5.1 %collective-permute-start.115 = (f32[8]{0:T(128)S(1)}, f32[8]{0:T(128)S(1)}, u32[]{:S(2)}, u32[]{:S(2)}) collective-permute-start(f32[8]{0:T(128)S(1)} %add_add_fusion.5), channel_id=1, source_target_pairs={{0,16},{1,17},{2,18},{3,19},{4,20},{5,21},{6,22},{7,23},{8,24},{9,... | collective-permute-start | bytes 104 | tf_op jit(solution)/shard_map/ppermute | solution.py:56
  391.6 19.6 %collective-permute-start.124 = (f32[8,3,1,4096]{3,2,0,1:T(1,128)S(1)}, f32[8,3,1,4096]{3,2,0,1:T(1,128)S(1)}, u32[]{:S(2)}, u32[]{:S(2)}) collective-permute-start(f32[8,3,1,4096]{3,2,0,1:T(1,128)S(1)} %get-tuple-element.225), channel_id=1, source_target_pairs={{0,1},{1,2},{2,3},{3,4},{4,5},{5,6},{6,7},{7,8},{8,9},{9,10},{10,1... | collective-permute-start | bytes 1179656 | tf_op jit(solution)/shard_map/ppermute | solution.py:22
  394.0 17.2 %collective-permute-start.125 = (f32[8,3,1,4096]{3,2,0,1:T(1,128)S(1)}, f32[8,3,1,4096]{3,2,0,1:T(1,128)S(1)}, u32[]{:S(2)}, u32[]{:S(2)}) collective-permute-start(f32[8,3,1,4096]{3,2,0,1:T(1,128)S(1)} %get-tuple-element.226), channel_id=1, source_target_pairs={{1,0},{2,1},{3,2},{4,3},{5,4},{6,5},{7,6},{8,7},{9,8},{10,9},{11,1... | collective-permute-start | bytes 1179656 | tf_op jit(solution)/shard_map/ppermute | solution.py:23
  398.1 5.1 %collective-permute-start.119 = (f32[8]{0:T(128)S(1)}, f32[8]{0:T(128)S(1)}, u32[]{:S(2)}, u32[]{:S(2)}) collective-permute-start(f32[8]{0:T(128)S(1)} %add.1110), channel_id=1, source_target_pairs={{0,4},{1,5},{2,6},{3,7},{4,0},{5,1},{6,2},{7,3},{8,12},{9,13},{10,... | collective-permute-start | bytes 104 | tf_op jit(solution)/shard_map/ppermute | solution.py:56
  406.0 5.1 %collective-permute-start.122 = (f32[8]{0:T(128)S(1)}, f32[8]{0:T(128)S(1)}, u32[]{:S(2)}, u32[]{:S(2)}) collective-permute-start(f32[8]{0:T(128)S(1)} %add_add_fusion.4), channel_id=1, source_target_pairs={{0,16},{1,17},{2,18},{3,19},{4,20},{5,21},{6,22},{7,23},{8,24},{9,... | collective-permute-start | bytes 104 | tf_op jit(solution)/shard_map/ppermute | solution.py:56
  426.2 5.1 %collective-permute-start.128 = (f32[8]{0:T(128)S(1)}, f32[8]{0:T(128)S(1)}, u32[]{:S(2)}, u32[]{:S(2)}) collective-permute-start(f32[8]{0:T(128)S(1)} %add.1119), channel_id=1, source_target_pairs={{0,4},{1,5},{2,6},{3,7},{4,0},{5,1},{6,2},{7,3},{8,12},{9,13},{10,... | collective-permute-start | bytes 104 | tf_op jit(solution)/shard_map/ppermute | solution.py:56
  433.7 5.1 %collective-permute-start.131 = (f32[8]{0:T(128)S(1)}, f32[8]{0:T(128)S(1)}, u32[]{:S(2)}, u32[]{:S(2)}) collective-permute-start(f32[8]{0:T(128)S(1)} %add_add_fusion.2), channel_id=1, source_target_pairs={{0,16},{1,17},{2,18},{3,19},{4,20},{5,21},{6,22},{7,23},{8,24},{9,... | collective-permute-start | bytes 104 | tf_op jit(solution)/shard_map/ppermute | solution.py:56
  442.5 5.1 %collective-permute-start.135 = (f32[8,6]{0,1:T(8,128)S(1)}, f32[8,6]{0,1:T(8,128)S(1)}, u32[]{:S(2)}, u32[]{:S(2)}) collective-permute-start(f32[8,6]{0,1:T(8,128)S(1)} %add.1133), channel_id=1, source_target_pairs={{0,4},{1,5},{2,6},{3,7},{4,0},{5,1},{6,2},{7,3},{8,12},{9,13},{10,... | collective-permute-start | bytes 584 | tf_op jit(solution)/shard_map/ppermute | solution.py:56
  448.7 5.1 %collective-permute-start.138 = (f32[8,6]{0,1:T(8,128)S(1)}, f32[8,6]{0,1:T(8,128)S(1)}, u32[]{:S(2)}, u32[]{:S(2)}) collective-permute-start(f32[8,6]{0,1:T(8,128)S(1)} %add_add_fusion.1), channel_id=1, source_target_pairs={{0,16},{1,17},{2,18},{3,19},{4,20},{5,21},{6,22},{7,23},{8,24},{9,... | collective-permute-start | bytes 584 | tf_op jit(solution)/shard_map/ppermute | solution.py:56
  458.1 5.1 %collective-permute-start.141 = (f32[4,6]{0,1:T(8,128)S(1)}, f32[4,6]{0,1:T(8,128)S(1)}, u32[]{:S(2)}, u32[]{:S(2)}) collective-permute-start(f32[4,6]{0,1:T(8,128)S(1)} %get-tuple-element.300), channel_id=1, source_target_pairs={{0,64},{32,96},{64,0},{96,32},{1,65},{33,97},{65,1},{97,33},{2,66}... | collective-permute-start | bytes 296 | tf_op jit(solution)/shard_map/ppermute | solution.py:81
  (82 other events, 328.5 us)
